TPU v7x, 32 devices: a whole 2x2x4 slice. The times are simulated.
32 devices in a mesh: cache: 8 (over z, x), stream: 4 (over y, core).
Axes of the slice: x: 2, y: 2, z: 4, core: 2. Of those that a mesh axis runs over, the one named last changes fastest.
Arguments:
- queries: bfloat16 [2048, 4096], P('cache', 'stream'), may hold values from -12.5 to 12.5
- own_kv: bfloat16 [2048, 1024], P('cache', 'stream'), may hold values from -6 to 6
- passage_store: bfloat16 [128, 512, 1024], P('cache', None, 'stream'), may hold values from -6 to 6
- out_weight: bfloat16 [4096, 8192], P('stream', 'cache'), may hold values from -0.375 to 0.375
- passage_slot: int32 [128], replicated, may hold values from 0 to 127, as said below
- retrieved: int32 [16, 16], P('cache'), may hold values from 0 to 127, as said below
Outputs:
- layer_out: bfloat16 [2048, 8192], P('cache', 'stream')
Inputs may be any that keep to these rules, and one draw needn't show every extreme that they name: `passage_slot`: a permutation. `retrieved`: over the 2 queries of one index of cache all ids are distinct; at most 8 of their slots fall in any one block of 16 consecutive slots, and some block holds exactly 8 of them for every index of cache.
All inputs are finite; a program needn't handle non-finite values.
Results may differ from a plain program's by a relative error of at most 0.015.
Values may be sent and summed in bfloat16 or wider, within the bound.
No kernel may reach another device: no remote copies, remote signals or barrier semaphores. Data moves between devices by JAX's collectives and lax.ppermute only.
A program may use at most 192 MiB of HBM per device.

v0:
```python
import math
import jax
import jax.numpy as jnp
from jax import lax
from jax.sharding import PartitionSpec as P

HD = 128
QLEN = 128
PLEN = 512


def attend_query(query_rows, own_rows, passages):
    kv_count = own_rows.shape[1] // (2 * HD)
    groups = query_rows.shape[1] // (kv_count * HD)
    tokens_here = query_rows.shape[0]
    passage_len = passages.shape[0]
    length = passage_len + tokens_here
    context = jnp.concatenate([passages, own_rows], axis=0).reshape(length, kv_count, 2, HD)
    key_part = context[:, :, 0, :]
    value_part = context[:, :, 1, :]
    query_part = query_rows.reshape(tokens_here, kv_count, groups, HD)
    scores = jnp.einsum(
        "tkgd,lkd->kgtl", query_part, key_part, preferred_element_type=jnp.float32
    ) / math.sqrt(HD)
    position = jnp.arange(length)[None, :] - passage_len
    visible = position <= jnp.arange(tokens_here)[:, None]
    scores = jnp.where(visible, scores, -jnp.inf)
    row_peak = jnp.max(scores, axis=-1, keepdims=True)
    powers = jnp.exp(scores - row_peak)
    totals = jnp.sum(powers, axis=-1)
    soft_weights = powers.astype(jnp.bfloat16)
    weighted = jnp.einsum(
        "kgtl,lkd->tkgd", soft_weights, value_part, preferred_element_type=jnp.float32
    )
    attended = weighted / jnp.transpose(totals, (2, 0, 1))[..., None]
    return attended.reshape(tokens_here, kv_count * groups * HD).astype(jnp.bfloat16)


def shards(queries, own_kv, passage_store, out_weight, passage_slot, retrieved):
    n_cache = lax.axis_size("cache")
    store_count = passage_store.shape[0]
    width_kv = passage_store.shape[2]
    slot_total = passage_slot.shape[0]
    query_count, per_query = retrieved.shape
    wanted_count = query_count * per_query
    capacity = max(2, (2 * wanted_count + n_cache - 1) // n_cache)
    wanted = retrieved.reshape(wanted_count)
    id_match = wanted[:, None] == jnp.arange(slot_total, dtype=jnp.int32)[None, :]
    store_slots = jnp.sum(jnp.where(id_match, passage_slot[None, :], 0), axis=1)
    owners = store_slots // store_count
    local_rows = store_slots % store_count
    places = jnp.arange(wanted_count, dtype=jnp.int32)
    earlier = (owners[None, :] == owners[:, None]) & (places[None, :] < places[:, None])
    order_rank = jnp.sum(earlier, axis=1)
    flat_slot = owners * capacity + order_rank
    slot_match = flat_slot[:, None] == jnp.arange(n_cache * capacity, dtype=jnp.int32)[None, :]
    send_rows = jnp.sum(jnp.where(slot_match, local_rows[:, None], 0), axis=0).reshape(
        n_cache, capacity
    )
    asked_rows = lax.all_to_all(send_rows, "cache", split_axis=0, concat_axis=0, tiled=True)
    outgoing = passage_store[asked_rows]
    arrived = lax.all_to_all(outgoing, "cache", split_axis=0, concat_axis=0, tiled=True)
    picked = arrived.reshape(n_cache * capacity, PLEN, width_kv)[flat_slot]

    def per_query_block(inputs):
        query_rows, own_rows, passages = inputs
        return attend_query(query_rows, own_rows, passages)

    attended = lax.map(
        per_query_block,
        (
            queries.reshape(query_count, QLEN, queries.shape[1]),
            own_kv.reshape(query_count, QLEN, own_kv.shape[1]),
            picked.reshape(query_count, per_query * PLEN, width_kv),
        ),
    )
    attended = attended.reshape(query_count * QLEN, queries.shape[1])
    return project(attended, out_weight)


def project(attended, out_weight):
    n_cache = lax.axis_size("cache")
    n_stream = lax.axis_size("stream")
    rows = attended.shape[0]
    group = n_cache // n_stream
    everyone = lax.all_gather(attended, "cache", axis=0, tiled=True)
    partial_sums = jnp.dot(everyone, out_weight, preferred_element_type=jnp.float32)
    reduced = lax.psum_scatter(
        partial_sums.astype(jnp.bfloat16), "stream", scatter_dimension=0, tiled=True
    )
    me = lax.axis_index("cache")
    width = reduced.shape[1]
    out = jnp.zeros((rows, group * width), reduced.dtype)
    for r in range(group):
        take = (me % group + r) % group
        piece = lax.dynamic_slice_in_dim(reduced, take * rows, rows, axis=0)
        perm = []
        for c in range(n_cache):
            for s in range(n_stream):
                dst_c = s * group + (c % group + r) % group
                dst_s = c // group
                perm.append((c * n_stream + s, dst_c * n_stream + dst_s))
        got = lax.ppermute(piece, ("cache", "stream"), perm)
        put = (me - r) % group
        out = lax.dynamic_update_slice_in_dim(out, got, put * width, axis=1)
    return out


def solution(mesh):
    return jax.shard_map(
        shards,
        mesh=mesh,
        in_specs=(
            P("cache", "stream"),
            P("cache", "stream"),
            P("cache", None, "stream"),
            P("stream", "cache"),
            P(),
            P("cache", None),
        ),
        out_specs=P("cache", "stream"),
        check_vma=False,
    )
```

profile of v0, /device:TPU:4, one launch (start us, length us, event | category | flops | bytes accessed | tf_op | source)
XLA Modules:
  0.0 729.6 jit_solution(13120011358236367580)
XLA Ops:
  6.5 0.0 copy-start
  6.5 0.9 eq.50
  7.4 0.8 select_reduce_fusion.1
  8.3 0.2 convert_reduce_fusion
  8.5 0.1 select_reduce_fusion
  8.6 0.1 all_to_all.11
  8.7 12.1 %all_to_all.17 = s32[8,1,8]{2,1,0:T(1,128)S(1)} all-to-all(s32[8,1,8]{2,1,0:T(1,128)S(1)} %bitcast.128), channel_id=1, replica_groups=mesh['cache'=8,'stream'=4] {'cache'}, dimensions={0} | all-to-all | bytes 512 | tf_op jit(solution)/shard_map/all_to_all | solution.py:60
  20.7 0.1 reshape.245
  20.8 9.6 %gather_fusion = bf16[64,512,256]{2,1,0:T(8,128)(2,1)} fusion(bf16[16,512,256]{2,1,0:T(8,128)(2,1)} %param.10, s32[1024]{0:T(1024)S(1)} %pad_clamp_fusion.1), kind=kCustom, calls=%fused_computation | custom fusion | bytes 33554688 | tf_op jit(solution)/shard_map/gather | solution.py:61
  30.4 5.8 all-to-all-start.1
  36.2 0.0 all-gather.2.cloned.1.call-start
  36.2 361.6 %all-to-all-done.1 = bf16[8,8,512,256]{3,2,1,0:T(8,128)(2,1)} async-done(((bf16[8,8,512,256]{3,2,1,0:T(8,128)(2,1)}), bf16[8,8,512,256]{3,2,1,0:T(8,128)(2,1)}, u32[]{:S(2)}, u32[]{:S(2)}) %all-to-all-start.1) | async-done | bytes 16777248 | tf_op jit(solution)/shard_map/all_to_all | solution.py:62
  397.8 0.0 copy-start.1
  397.8 0.0 copy-start.3
  397.8 10.9 %gather_fusion.1 = bf16[32,512,256]{2,1,0:T(8,128)(2,1)} fusion(bf16[64,512,256]{2,1,0:T(8,128)(2,1)} %bitcast.19, s32[1024]{0:T(1024)S(1)} %pad_clamp_fusion), kind=kCustom, calls=%fused_computation.1 | custom fusion | bytes 16777344 | tf_op jit(solution)/shard_map/gather | solution.py:63
  408.7 0.0 copy-done.1
  408.7 0.0 copy-done.3
  408.7 135.2 %while.12 = (s32[]{:T(128)}, bf16[2,128,1024]{2,1,0:T(8,128)(2,1)}, bf16[2,8192,256]{2,1,0:T(8,128)(2,1)}, bf16[2,128,256]{2,1,0:T(8,128)(2,1)S(1)}, bf16[2,128,1024]{2,1,0:T(8,128)(2,1)S(1)}, /*index=5*/s32[]{:T(128)}) while((s32[]{:T(128)}, bf16[2,128,1024]{2,1,0:T(8,128)(2,1)}, bf16[2,8192,256]{2,1,0:T(8,128)(2,1)}, ...), condition=%wide.region_6.7_spmd, body=%wide.region_3.6_spmd.sunk | while | flops 4465645568 | bytes 143283808 | solution.py:69
  408.7 4.4 constant_dynamic-slice_fusion.10
  413.1 6.4 copy.62
  419.6 6.3 copy.63
  425.9 0.1 copy.60
  426.0 0.1 copy.61
  426.2 0.2 copy.59
  426.4 3.8 iota_compare_fusion.5
  430.2 14.9 %fusion.47 = (f32[8,128]{1,0:T(8,128)S(1)}, f32[8320,128,8]{1,0,2:T(8,128)}) fusion(pred[128,8320]{0,1:T(8,128)(4,1)S(1)} %iota_compare_fusion.5, bf16[128,8,128]{0,2,1:T(8,128)(2,1)S(1)} %bitcast.121, bf16[128,1,2,128]{3,0,2,1:T(8,128)(2,1)S(1)} %copy.61, bf16[8192,1,2,128]{3,0,2,1:T(8,128)(2,1)} %copy.63), kind=kOutput, calls=%fused_computation.6.clone.1 | convolution fusion | flops 2210855936 | bytes 39669760 | tf_op jit(solution)/shard_map/while/body/eval_jaxpr/tkgd,lkd->kgtl/dot_general | solution.py:22
  445.0 14.4 %fusion.48 = f32[8,128]{1,0:T(8,128)S(1)} fusion(f32[8320,128,8]{1,0,2:T(8,128)} %get-tuple-element.135, f32[8,128]{1,0:T(8,128)S(1)} %get-tuple-element.136, pred[128,8320]{0,1:T(8,128)(4,1)S(1)} %iota_compare_fusion.5), kind=kLoop, calls=%fused_computation.4.clone.1 | loop fusion | flops 34077696 | bytes 35151872 | tf_op jit(solution)/shard_map/while/body/eval_jaxpr/reduce_sum | solution.py:30
  459.4 16.1 %fusion.49 = bf16[128,1,8,128]{0,3,2,1:T(8,128)(2,1)S(1)} fusion(f32[8320,128,8]{1,0,2:T(8,128)} %get-tuple-element.135, f32[8,128]{1,0:T(8,128)S(1)} %get-tuple-element.136, pred[128,8320]{0,1:T(8,128)(4,1)S(1)} %iota_compare_fusion.5, bf16[8192,1,2,128]{3,0,2,1:T(8,128)(2,1)} %copy.63, bf16[128,1,2,128]{3,0,2,1:T(8,128)(2,1)S(1)} %copy.61, ...), kind=kOutput, calls=%fused_computation.21.clone.1 | convolution fusion | flops 2219638784 | bytes 39673856 | tf_op jit(solution)/shard_map/while/body/eval_jaxpr/kgtl,lkd->tkgd/dot_general | solution.py:32
  475.5 0.1 copy.64
  475.6 0.7 constant_dynamic-update-slice_fusion.4
  476.3 4.4 constant_dynamic-slice_fusion.10
  480.8 6.4 copy.62
  487.2 6.3 copy.63
  493.5 0.1 copy.60
  493.6 0.1 copy.61
  493.8 0.2 copy.59
  494.0 3.8 iota_compare_fusion.5
  497.8 14.9 %fusion.47 = (f32[8,128]{1,0:T(8,128)S(1)}, f32[8320,128,8]{1,0,2:T(8,128)}) fusion(pred[128,8320]{0,1:T(8,128)(4,1)S(1)} %iota_compare_fusion.5, bf16[128,8,128]{0,2,1:T(8,128)(2,1)S(1)} %bitcast.121, bf16[128,1,2,128]{3,0,2,1:T(8,128)(2,1)S(1)} %copy.61, bf16[8192,1,2,128]{3,0,2,1:T(8,128)(2,1)} %copy.63), kind=kOutput, calls=%fused_computation.6.clone.1 | convolution fusion | flops 2210855936 | bytes 39669760 | tf_op jit(solution)/shard_map/while/body/eval_jaxpr/tkgd,lkd->kgtl/dot_general | solution.py:22
  512.6 14.4 %fusion.48 = f32[8,128]{1,0:T(8,128)S(1)} fusion(f32[8320,128,8]{1,0,2:T(8,128)} %get-tuple-element.135, f32[8,128]{1,0:T(8,128)S(1)} %get-tuple-element.136, pred[128,8320]{0,1:T(8,128)(4,1)S(1)} %iota_compare_fusion.5), kind=kLoop, calls=%fused_computation.4.clone.1 | loop fusion | flops 34077696 | bytes 35151872 | tf_op jit(solution)/shard_map/while/body/eval_jaxpr/reduce_sum | solution.py:30
  527.0 16.1 %fusion.49 = bf16[128,1,8,128]{0,3,2,1:T(8,128)(2,1)S(1)} fusion(f32[8320,128,8]{1,0,2:T(8,128)} %get-tuple-element.135, f32[8,128]{1,0:T(8,128)S(1)} %get-tuple-element.136, pred[128,8320]{0,1:T(8,128)(4,1)S(1)} %iota_compare_fusion.5, bf16[8192,1,2,128]{3,0,2,1:T(8,128)(2,1)} %copy.63, bf16[128,1,2,128]{3,0,2,1:T(8,128)(2,1)S(1)} %copy.61, ...), kind=kOutput, calls=%fused_computation.21.clone.1 | convolution fusion | flops 2219638784 | bytes 39673856 | tf_op jit(solution)/shard_map/while/body/eval_jaxpr/kgtl,lkd->tkgd/dot_general | solution.py:32
  543.1 0.1 copy.64
  543.2 0.7 constant_dynamic-update-slice_fusion.4
  544.0 0.0 all-gather.2.cloned.1.call-update
  544.0 0.2 reduce-scatter.2.cloned.1.call-start
  544.2 72.3 %all-gather.2.cloned.1.call-done = bf16[2048,1024]{1,0:T(8,128)(2,1)} async-done(((bf16[256,1024]{1,0:T(8,128)(2,1)}), bf16[2048,1024]{1,0:T(8,128)(2,1)}) %all-gather.2.cloned.1.call-update) | async-done | bytes 4194320 | tf_op jit(solution)/shard_map/all_gather | solution.py:86
  616.5 0.0 copy-done
  616.5 8.3 %convolution_convert_fusion = bf16[2048,1024]{1,0:T(8,128)(2,1)} fusion(bf16[2048,1024]{1,0:T(8,128)(2,1)} %all-gather.2.cloned.1.call-done, bf16[1024,1024]{1,0:T(8,128)(2,1)S(1)} %copy-done), kind=kOutput, calls=%fused_computation.31 | convolution fusion | flops 4297064448 | bytes 10485760 | tf_op jit(solution)/shard_map/dot_general | solution.py:87
  624.9 0.0 reduce-scatter.2.cloned.1.call-update
  624.9 41.7 %reduce-scatter.2.cloned.1.call-done = bf16[512,1024]{1,0:T(8,128)(2,1)} async-done(((bf16[2048,1024]{1,0:T(8,128)(2,1)}), bf16[512,1024]{1,0:T(8,128)(2,1)}) %reduce-scatter.2.cloned.1.call-update) | async-done | bytes 1048592 | tf_op jit(solution)/shard_map/reduce_scatter | solution.py:88
  666.7 2.2 constant_dynamic-slice_fusion.3
  668.9 5.5 collective-permute-start
  674.4 1.5 collective-permute-start.1
  675.8 34.2 %collective-permute-done = bf16[256,1024]{1,0:T(8,128)(2,1)S(1)} collective-permute-done((bf16[256,1024]{1,0:T(8,128)(2,1)}, bf16[256,1024]{1,0:T(8,128)(2,1)S(1)}, u32[]{:S(2)}, u32[]{:S(2)}) %collective-permute-start) | collective-permute-done | bytes 524320 | tf_op jit(solution)/shard_map/ppermute | solution.py:103
  710.1 0.1 broadcast_in_dim.61
  710.2 0.1 constant_dynamic-update-slice_fusion.1
  710.2 0.0 copy-start.2
  710.3 11.6 %collective-permute-done.1 = bf16[256,1024]{1,0:T(8,128)(2,1)S(1)} collective-permute-done((bf16[256,1024]{1,0:T(8,128)(2,1)}, bf16[256,1024]{1,0:T(8,128)(2,1)S(1)}, u32[]{:S(2)}, u32[]{:S(2)}) %collective-permute-start.1) | collective-permute-done | bytes 524320 | tf_op jit(solution)/shard_map/ppermute | solution.py:103
  721.9 0.0 copy-done.2
  721.9 0.8 constant_dynamic-update-slice_fusion.2
  (13 shorter events, 0.1 us)
Async XLA Ops:
  6.5 610.0 %copy-start = (bf16[1024,1024]{1,0:T(8,128)(2,1)S(1)}, bf16[1024,1024]{1,0:T(8,128)(2,1)}, u32[]{:S(2)}) copy-start(bf16[1024,1024]{1,0:T(8,128)(2,1)} %param.11) | copy-start | bytes 6291460
  30.4 367.4 %all-to-all-start.1 = ((bf16[8,8,512,256]{3,2,1,0:T(8,128)(2,1)}), bf16[8,8,512,256]{3,2,1,0:T(8,128)(2,1)}, u32[]{:S(2)}, u32[]{:S(2)}) async-start(bf16[8,8,512,256]{3,2,1,0:T(8,128)(2,1)} %bitcast.120), calls=%async_computation.1 | async-start | bytes 33554432 | tf_op jit(solution)/shard_map/all_to_all | solution.py:62
  36.2 580.4 %all-gather.2.cloned.1.call-start = ((), (), s32[]{:S(2)}) async-start(), calls=%async_computation.3 | async-start | bytes 4718592 | tf_op jit(solution)/shard_map/all_gather | solution.py:86
  397.8 10.9 %copy-start.1 = (bf16[256,1024]{1,0:T(8,128)(2,1)S(1)}, bf16[256,1024]{1,0:T(8,128)(2,1)}, u32[]{:S(2)}) copy-start(bf16[256,1024]{1,0:T(8,128)(2,1)} %param.8) | copy-start | bytes 1572868
  397.8 10.9 %copy-start.3 = (bf16[256,256]{1,0:T(8,128)(2,1)S(1)}, bf16[256,256]{1,0:T(8,128)(2,1)}, u32[]{:S(2)}) copy-start(bf16[256,256]{1,0:T(8,128)(2,1)} %param.9) | copy-start | bytes 393220
  544.0 122.7 %reduce-scatter.2.cloned.1.call-start = ((), (), s32[]{:S(2)}) async-start(), calls=%async_computation.4 | async-start | bytes 5242880 | tf_op jit(solution)/shard_map/reduce_scatter | solution.py:88
  668.9 41.2 %collective-permute-start = (bf16[256,1024]{1,0:T(8,128)(2,1)}, bf16[256,1024]{1,0:T(8,128)(2,1)S(1)}, u32[]{:S(2)}, u32[]{:S(2)}) collective-permute-start(bf16[256,1024]{1,0:T(8,128)(2,1)} %get-tuple-element.99), channel_id=1, source_target_pairs={{0,0},{1,8},{2,16},{3,24},{4,4},{5,12},{6,20},{7,28},{8,1},{9,9},{... | collective-permute-start | bytes 1572872 | tf_op jit(solution)/shard_map/ppermute | solution.py:103
  674.4 47.5 %collective-permute-start.1 = (bf16[256,1024]{1,0:T(8,128)(2,1)}, bf16[256,1024]{1,0:T(8,128)(2,1)S(1)}, u32[]{:S(2)}, u32[]{:S(2)}) collective-permute-start(bf16[256,1024]{1,0:T(8,128)(2,1)} %get-tuple-element.98), channel_id=1, source_target_pairs={{0,4},{1,12},{2,20},{3,28},{4,0},{5,8},{6,16},{7,24},{8,5},{9,13},... | collective-permute-start | bytes 1572872 | tf_op jit(solution)/shard_map/ppermute | solution.py:103
  710.2 11.6 %copy-start.2 = (bf16[256,2048]{1,0:T(8,128)(2,1)}, bf16[256,2048]{1,0:T(8,128)(2,1)S(1)}, u32[]{:S(2)}) copy-start(bf16[256,2048]{1,0:T(8,128)(2,1)S(1)} %constant_dynamic-update-slice_fusion.1) | copy-start | bytes 3145732
Sparse Core Ops, SparseCore 0:
  544.1 72.3 all-gather.1
  625.0 41.6 reduce-scatter.1
where the time goes:
time: 731 us; the launch traced here: 730 us
  waiting for transfers between devices  522 us (71%)
  matrix products  70.2 us (10%)
  local copies, waits for them, and re-layouts  61.7 us (8%)
  other arithmetic  37.4 us (5%)
  between operations  13.5 us (2%)
  starting transfers between devices  12.9 us (2%)
  blocking collectives  12.1 us (2%)
    all_to_all x1, waiting for transfers between devices, shards(): lax.all_to_all(outgoing, 'cache', split_axis=0, concat_axis=0, tiled=True)  362 us
    all_gather x1, waiting for transfers between devices, project(): everyone = lax.all_gather(attended, 'cache', axis=0, tiled=True)  72.3 us
    ppermute x2, waiting for transfers between devices, project(): got = lax.ppermute(piece, ('cache', 'stream'), perm)  45.9 us
    reduce_scatter x1, waiting for transfers between devices, project(): lax.psum_scatter(partial_sums.astype(jnp.bfloat16), 'stream', scatter_dim...  41.7 us
    dot_general x2, matrix products, attend_query(): jnp.einsum('kgtl,lkd->tkgd', soft_weights, value_part, preferred_element_...  32.1 us
    dot_general x2, matrix products, attend_query(): jnp.einsum('tkgd,lkd->kgtl', query_part, key_part, preferred_element_type...  29.7 us
    reduce_sum x2, other arithmetic, attend_query(): totals = jnp.sum(powers, axis=-1)  28.7 us
    dynamic_slice x12, local copies, waits for them, and re-layouts, shards(): lax.map(per_query_block, (queries.reshape(query_count, QLEN, queries.shap...  22.3 us
  transfers between devices with their start and end apart: 5, of which 5 were waited for; matrix products, arithmetic and copies ran while one was open for 0% of the time, Pallas kernels for 0%

commit v1 on v0

--- a/solution.py
+++ b/solution.py
@@ -7,6 +7,17 @@
 HD = 128
 QLEN = 128
 PLEN = 512
+
+
+def in_blocks(value, dim, size):
+    before, after = (value.shape[:dim], value.shape[dim + 1 :])
+    return jnp.moveaxis(value.reshape(*before, size, -1, *after), dim, 0)
+
+
+def in_order(tiles, dim):
+    tiles = jnp.moveaxis(tiles, 0, dim)
+    shape = tiles.shape
+    return tiles.reshape(*shape[:dim], shape[dim] * shape[dim + 1], *shape[dim + 2 :])
 
 
 def attend_query(query_rows, own_rows, passages):
@@ -59,7 +70,14 @@
     )
     asked_rows = lax.all_to_all(send_rows, "cache", split_axis=0, concat_axis=0, tiled=True)
     outgoing = passage_store[asked_rows]
-    arrived = lax.all_to_all(outgoing, "cache", split_axis=0, concat_axis=0, tiled=True)
+    size, place = (lax.axis_size("cache"), lax.axis_index("cache"))
+    pieces = in_blocks(outgoing, 0, size)
+    outs = [pieces[place]]
+    for lap in range(1, size):
+        sent = pieces[place ^ lap]
+        outs.append(lax.ppermute(sent, "cache", [(i, i ^ lap) for i in range(size)]))
+    pieces = jnp.stack(outs)[place ^ jnp.arange(size)]
+    arrived = in_order(pieces, 0)
     picked = arrived.reshape(n_cache * capacity, PLEN, width_kv)[flat_slot]
 
     def per_query_block(inputs):

time: 731 us -> 775 us (1.060)
  local copies, waits for them, and re-layouts: 61.7 us -> 106 us
  other arithmetic: 37.4 us -> 51 us
  blocking collectives: 12.1 us -> 0 us
  waiting for transfers between devices: 522 us -> 510 us
  starting transfers between devices: 12.9 us -> 22.6 us
    all_to_all x1, waiting for transfers between devices: 362 us -> 6.3 us  [shards(): lax.all_to_all(send_rows, 'cache', split_axis=0, concat_axis=0, tiled=True)]
    ppermute x0 -> x7, waiting for transfers between devices: none -> 259 us  [shards(): lax.ppermute(sent, 'cache', [(i, i ^ lap) for i in range(size)])]
    all_gather x1, waiting for transfers between devices: 72.3 us -> 156 us  [project(): everyone = lax.all_gather(attended, 'cache', axis=0, tiled=True)]
    gather x0 -> x3, local copies, waits for them, and re-layouts: none -> 22.3 us  [shards(): pieces = jnp.stack(outs)[place ^ jnp.arange(size)]]
    unnamed x0 -> x1, other arithmetic: none -> 13.5 us
    all_to_all x1 -> x0, blocking collectives: 12.1 us -> none  [shards(): lax.all_to_all(send_rows, 'cache', split_axis=0, concat_axis=0, tiled=True)]
    squeeze x0 -> x1, local copies, waits for them, and re-layouts: none -> 10.7 us  [shards(): sent = pieces[place ^ lap]]
    unnamed x8 -> x15, local copies, waits for them, and re-layouts: 0.02 us -> 10.6 us
  transfers between devices with their start and end apart: 5 -> 12, of which waited for: 5 -> 9; matrix products, arithmetic and copies ran while one was open for 0% -> 1% of each run, Pallas kernels for 0% -> 0%
where the time goes in v1:
time: 775 us; the launch traced here: 773 us
  waiting for transfers between devices  510 us (66%)
  local copies, waits for them, and re-layouts  106 us (14%)
  matrix products  70.2 us (9%)
  other arithmetic  51 us (7%)
  starting transfers between devices  22.6 us (3%)
  between operations  13.6 us (2%)
    ppermute x7, waiting for transfers between devices, shards(): lax.ppermute(sent, 'cache', [(i, i ^ lap) for i in range(size)])  259 us
    all_gather x1, waiting for transfers between devices, project(): everyone = lax.all_gather(attended, 'cache', axis=0, tiled=True)  156 us
    ppermute x2, waiting for transfers between devices, project(): got = lax.ppermute(piece, ('cache', 'stream'), perm)  45.9 us
    reduce_scatter x1, waiting for transfers between devices, project(): lax.psum_scatter(partial_sums.astype(jnp.bfloat16), 'stream', scatter_dim...  41.7 us
    dot_general x2, matrix products, attend_query(): jnp.einsum('kgtl,lkd->tkgd', soft_weights, value_part, preferred_element_...  32.1 us
    dot_general x2, matrix products, attend_query(): jnp.einsum('tkgd,lkd->kgtl', query_part, key_part, preferred_element_type...  29.8 us
    reduce_sum x2, other arithmetic, attend_query(): totals = jnp.sum(powers, axis=-1)  28.7 us
    gather x3, local copies, waits for them, and re-layouts, shards(): pieces = jnp.stack(outs)[place ^ jnp.arange(size)]  22.3 us
  transfers between devices with their start and end apart: 12, of which 9 were waited for; matrix products, arithmetic and copies ran while one was open for 1% of the time, Pallas kernels for 0%

profile of v1, /device:TPU:4, one launch (start us, length us, event | category | flops | bytes accessed | tf_op | source)
XLA Modules:
  0.0 773.2 jit_solution(4978737872284901018)
XLA Ops:
  6.5 0.9 eq.50
  7.4 0.8 select_reduce_fusion.1
  8.3 0.2 convert_reduce_fusion
  8.6 0.7 all_to_all.8
  9.3 5.8 all-to-all-start
  15.2 6.3 all-to-all-done
  21.6 9.6 %gather_fusion = bf16[64,512,256]{2,1,0:T(8,128)(2,1)} fusion(bf16[16,512,256]{2,1,0:T(8,128)(2,1)} %param.10, s32[1024]{0:T(1024)S(1)} %pad_clamp_fusion.2), kind=kCustom, calls=%fused_computation | custom fusion | bytes 33554688 | tf_op jit(solution)/shard_map/gather | solution.py:72
  31.2 10.7 %constant_dynamic-slice_fusion.5 = (bf16[1,8,512,256]{3,2,1,0:T(8,128)(2,1)}, bf16[1,8,512,256]{3,2,1,0:T(8,128)(2,1)}, bf16[1,8,512,256]{3,2,1,0:T(8,128)(2,1)}...) fusion(bf16[8,8,512,256]{3,2,1,0:T(8,128)(2,1)} %bitcast.144, ...), kind=kLoop, calls=%fused_computation.59 | loop fusion | bytes 29360156 | tf_op jit(solution)/shard_map/squeeze | solution.py:77
  41.9 0.6 collective-permute-start
  42.4 0.5 collective-permute-start.1
  43.0 2.4 collective-permute-start.2
  45.4 0.5 collective-permute-start.3
  45.9 2.4 collective-permute-start.4
  48.3 39.9 %collective-permute-done = bf16[1,8,512,256]{3,2,1,0:T(8,128)(2,1)} collective-permute-done((bf16[1,8,512,256]{3,2,1,0:T(8,128)(2,1)}, bf16[1,8,512,256]{3,2,1,0:T(8,128)(2,1)}, u32[]{:S(2)}, u32[]{:S(2)}) %collective-permute-start) | collective-permute-done | bytes 2097184 | tf_op jit(solution)/shard_map/ppermute | solution.py:78
  88.2 0.7 collective-permute-start.5
  88.9 88.9 %collective-permute-done.1 = bf16[1,8,512,256]{3,2,1,0:T(8,128)(2,1)} collective-permute-done((bf16[1,8,512,256]{3,2,1,0:T(8,128)(2,1)}, bf16[1,8,512,256]{3,2,1,0:T(8,128)(2,1)}, u32[]{:S(2)}, u32[]{:S(2)}) %collective-permute-start.1) | collective-permute-done | bytes 2097184 | tf_op jit(solution)/shard_map/ppermute | solution.py:78
  177.9 2.6 collective-permute-start.6
  180.5 1.7 bitcast_dynamic-update-slice_fusion.7
  182.2 1.7 bitcast_dynamic-update-slice_fusion.6
  184.0 1.7 bitcast_dynamic-update-slice_fusion.5
  185.7 35.6 %collective-permute-done.2 = bf16[1,8,512,256]{3,2,1,0:T(8,128)(2,1)} collective-permute-done((bf16[1,8,512,256]{3,2,1,0:T(8,128)(2,1)}, bf16[1,8,512,256]{3,2,1,0:T(8,128)(2,1)}, u32[]{:S(2)}, u32[]{:S(2)}) %collective-permute-start.2) | collective-permute-done | bytes 2097184 | tf_op jit(solution)/shard_map/ppermute | solution.py:78
  221.3 1.7 bitcast_dynamic-update-slice_fusion.4
  223.1 1.7 bitcast_dynamic-update-slice_fusion.3
  224.8 95.0 %collective-permute-done.4 = bf16[1,8,512,256]{3,2,1,0:T(8,128)(2,1)} collective-permute-done((bf16[1,8,512,256]{3,2,1,0:T(8,128)(2,1)}, bf16[1,8,512,256]{3,2,1,0:T(8,128)(2,1)}, u32[]{:S(2)}, u32[]{:S(2)}) %collective-permute-start.4) | collective-permute-done | bytes 2097184 | tf_op jit(solution)/shard_map/ppermute | solution.py:78
  319.9 1.7 bitcast_dynamic-update-slice_fusion.2
  321.6 0.1 bitcast_dynamic-update-slice_fusion.1
  321.8 0.1 bitcast_dynamic-update-slice_fusion
  321.9 6.2 slice_bitcast_fusion.1
  328.1 8.1 %gather_fusion.2 = bf16[8,8,256,256]{3,2,1,0:T(8,128)(2,1)} fusion(bf16[8,8,256,256]{3,2,1,0:T(8,128)(2,1)} %get-tuple-element.98, s32[1024]{0:T(1024)S(1)} %get-tuple-element.112), kind=kCustom, calls=%fused_computation.2 | custom fusion | bytes 16777248 | tf_op jit(solution)/shard_map/gather | solution.py:79
  336.2 8.1 %gather_fusion.3 = bf16[8,8,256,256]{3,2,1,0:T(8,128)(2,1)} fusion(bf16[8,8,256,256]{3,2,1,0:T(8,128)(2,1)} %get-tuple-element.99, s32[1024]{0:T(1024)S(1)} %get-tuple-element.112), kind=kCustom, calls=%fused_computation.3 | custom fusion | bytes 16777248 | tf_op jit(solution)/shard_map/gather | solution.py:79
  344.3 13.5 %pad_maximum_fusion.1 = bf16[8,1,8,512,256]{4,3,2,0,1:T(8,128)(2,1)} fusion(bf16[8,1,8,256,256]{4,3,2,0,1:T(8,128)(2,1)} %bitcast.148, bf16[8,1,8,256,256]{4,3,2,0,1:T(8,128)(2,1)} %bitcast.147), kind=kLoop, calls=%fused_computation.33 | loop fusion | flops 33554432 | bytes 33554432
  357.8 10.9 %gather_fusion.1 = bf16[32,512,256]{2,1,0:T(8,128)(2,1)} fusion(bf16[64,512,256]{2,1,0:T(8,128)(2,1)} %bitcast.146, s32[1024]{0:T(1024)S(1)} %get-tuple-element.111), kind=kCustom, calls=%fused_computation.1 | custom fusion | bytes 16777344 | tf_op jit(solution)/shard_map/gather | solution.py:81
  368.7 135.3 %while.12 = (s32[]{:T(128)}, bf16[2,128,1024]{2,1,0:T(8,128)(2,1)}, bf16[2,8192,256]{2,1,0:T(8,128)(2,1)}, bf16[2,128,256]{2,1,0:T(8,128)(2,1)S(1)}, bf16[2,128,1024]{2,1,0:T(8,128)(2,1)S(1)}, /*index=5*/s32[]{:T(128)}) while((s32[]{:T(128)}, bf16[2,128,1024]{2,1,0:T(8,128)(2,1)}, bf16[2,8192,256]{2,1,0:T(8,128)(2,1)}, ...), condition=%wide.region_6.7_spmd, body=%wide.region_3.6_spmd.sunk | while | flops 4465645568 | bytes 143283808 | solution.py:87
  368.7 4.4 constant_dynamic-slice_fusion.17
  373.1 6.4 copy.62
  379.6 6.3 copy.63
  386.0 0.1 copy.61
  386.2 0.2 copy.59
  386.4 3.8 iota_compare_fusion.5
  390.2 14.9 %fusion.48 = (f32[8,128]{1,0:T(8,128)S(1)}, f32[8320,128,8]{1,0,2:T(8,128)}) fusion(pred[128,8320]{0,1:T(8,128)(4,1)S(1)} %iota_compare_fusion.5, bf16[128,8,128]{0,2,1:T(8,128)(2,1)S(1)} %bitcast.149, bf16[128,1,2,128]{3,0,2,1:T(8,128)(2,1)S(1)} %copy.61, bf16[8192,1,2,128]{3,0,2,1:T(8,128)(2,1)} %copy.63), kind=kOutput, calls=%fused_computation.8.clone.1 | convolution fusion | flops 2210855936 | bytes 39669760 | tf_op jit(solution)/shard_map/while/body/eval_jaxpr/tkgd,lkd->kgtl/dot_general | solution.py:33
  405.1 14.4 %fusion.49 = f32[8,128]{1,0:T(8,128)S(1)} fusion(f32[8320,128,8]{1,0,2:T(8,128)} %get-tuple-element.146, f32[8,128]{1,0:T(8,128)S(1)} %get-tuple-element.147, pred[128,8320]{0,1:T(8,128)(4,1)S(1)} %iota_compare_fusion.5), kind=kLoop, calls=%fused_computation.6.clone.1 | loop fusion | flops 34077696 | bytes 35151872 | tf_op jit(solution)/shard_map/while/body/eval_jaxpr/reduce_sum | solution.py:41
  419.4 16.1 %fusion.50 = bf16[128,1,8,128]{0,3,2,1:T(8,128)(2,1)S(1)} fusion(f32[8320,128,8]{1,0,2:T(8,128)} %get-tuple-element.146, f32[8,128]{1,0:T(8,128)S(1)} %get-tuple-element.147, pred[128,8320]{0,1:T(8,128)(4,1)S(1)} %iota_compare_fusion.5, bf16[8192,1,2,128]{3,0,2,1:T(8,128)(2,1)} %copy.63, bf16[128,1,2,128]{3,0,2,1:T(8,128)(2,1)S(1)} %copy.61, ...), kind=kOutput, calls=%fused_computation.23.clone.1 | convolution fusion | flops 2219638784 | bytes 39673856 | tf_op jit(solution)/shard_map/while/body/eval_jaxpr/kgtl,lkd->tkgd/dot_general | solution.py:43
  435.5 0.1 copy.64
  435.6 0.7 constant_dynamic-update-slice_fusion.4
  436.4 4.4 constant_dynamic-slice_fusion.17
  440.8 6.4 copy.62
  447.2 6.3 copy.63
  453.7 0.1 copy.61
  453.9 0.2 copy.59
  454.0 3.8 iota_compare_fusion.5
  457.8 14.9 %fusion.48 = (f32[8,128]{1,0:T(8,128)S(1)}, f32[8320,128,8]{1,0,2:T(8,128)}) fusion(pred[128,8320]{0,1:T(8,128)(4,1)S(1)} %iota_compare_fusion.5, bf16[128,8,128]{0,2,1:T(8,128)(2,1)S(1)} %bitcast.149, bf16[128,1,2,128]{3,0,2,1:T(8,128)(2,1)S(1)} %copy.61, bf16[8192,1,2,128]{3,0,2,1:T(8,128)(2,1)} %copy.63), kind=kOutput, calls=%fused_computation.8.clone.1 | convolution fusion | flops 2210855936 | bytes 39669760 | tf_op jit(solution)/shard_map/while/body/eval_jaxpr/tkgd,lkd->kgtl/dot_general | solution.py:33
  472.7 14.4 %fusion.49 = f32[8,128]{1,0:T(8,128)S(1)} fusion(f32[8320,128,8]{1,0,2:T(8,128)} %get-tuple-element.146, f32[8,128]{1,0:T(8,128)S(1)} %get-tuple-element.147, pred[128,8320]{0,1:T(8,128)(4,1)S(1)} %iota_compare_fusion.5), kind=kLoop, calls=%fused_computation.6.clone.1 | loop fusion | flops 34077696 | bytes 35151872 | tf_op jit(solution)/shard_map/while/body/eval_jaxpr/reduce_sum | solution.py:41
  487.1 16.1 %fusion.50 = bf16[128,1,8,128]{0,3,2,1:T(8,128)(2,1)S(1)} fusion(f32[8320,128,8]{1,0,2:T(8,128)} %get-tuple-element.146, f32[8,128]{1,0:T(8,128)S(1)} %get-tuple-element.147, pred[128,8320]{0,1:T(8,128)(4,1)S(1)} %iota_compare_fusion.5, bf16[8192,1,2,128]{3,0,2,1:T(8,128)(2,1)} %copy.63, bf16[128,1,2,128]{3,0,2,1:T(8,128)(2,1)S(1)} %copy.61, ...), kind=kOutput, calls=%fused_computation.23.clone.1 | convolution fusion | flops 2219638784 | bytes 39673856 | tf_op jit(solution)/shard_map/while/body/eval_jaxpr/kgtl,lkd->tkgd/dot_general | solution.py:43
  503.1 0.1 copy.64
  503.3 0.7 constant_dynamic-update-slice_fusion.4
  504.1 156.1 %all-gather.2.cloned.1.call-done = bf16[2048,1024]{1,0:T(8,128)(2,1)} async-done(((bf16[256,1024]{1,0:T(8,128)(2,1)}), bf16[2048,1024]{1,0:T(8,128)(2,1)}) %all-gather.2.cloned.1.call-update) | async-done | bytes 4194320 | tf_op jit(solution)/shard_map/all_gather | solution.py:104
  660.2 8.3 %convolution_convert_fusion = bf16[2048,1024]{1,0:T(8,128)(2,1)} fusion(bf16[2048,1024]{1,0:T(8,128)(2,1)} %all-gather.2.cloned.1.call-done, bf16[1024,1024]{1,0:T(8,128)(2,1)S(1)} %copy-done), kind=kOutput, calls=%fused_computation.36 | convolution fusion | flops 4297064448 | bytes 10485760 | tf_op jit(solution)/shard_map/dot_general | solution.py:105
  668.6 41.7 %reduce-scatter.2.cloned.1.call-done = bf16[512,1024]{1,0:T(8,128)(2,1)} async-done(((bf16[2048,1024]{1,0:T(8,128)(2,1)}), bf16[512,1024]{1,0:T(8,128)(2,1)}) %reduce-scatter.2.cloned.1.call-update) | async-done | bytes 1048592 | tf_op jit(solution)/shard_map/reduce_scatter | solution.py:106
  710.3 2.2 constant_dynamic-slice_fusion.3
  712.6 5.5 collective-permute-start.7
  718.1 1.5 collective-permute-start.8
  719.5 34.2 %collective-permute-done.7 = bf16[256,1024]{1,0:T(8,128)(2,1)S(1)} collective-permute-done((bf16[256,1024]{1,0:T(8,128)(2,1)}, bf16[256,1024]{1,0:T(8,128)(2,1)S(1)}, u32[]{:S(2)}, u32[]{:S(2)}) %collective-permute-start.7) | collective-permute-done | bytes 524320 | tf_op jit(solution)/shard_map/ppermute | solution.py:121
  753.9 11.6 %collective-permute-done.8 = bf16[256,1024]{1,0:T(8,128)(2,1)S(1)} collective-permute-done((bf16[256,1024]{1,0:T(8,128)(2,1)}, bf16[256,1024]{1,0:T(8,128)(2,1)S(1)}, u32[]{:S(2)}, u32[]{:S(2)}) %collective-permute-start.8) | collective-permute-done | bytes 524320 | tf_op jit(solution)/shard_map/ppermute | solution.py:121
  765.6 0.8 constant_dynamic-update-slice_fusion.2
  (35 shorter events, 0.8 us)
Async XLA Ops:
  6.5 653.7 %copy-start = (bf16[1024,1024]{1,0:T(8,128)(2,1)S(1)}, bf16[1024,1024]{1,0:T(8,128)(2,1)}, u32[]{:S(2)}) copy-start(bf16[1024,1024]{1,0:T(8,128)(2,1)} %param.11) | copy-start | bytes 6291460
  9.3 12.2 %all-to-all-start = ((s32[8,1,8]{2,1,0:T(1,128)}), s32[8,1,8]{2,1,0:T(1,128)S(1)}, u32[]{:S(2)}, u32[]{:S(2)}) async-start(s32[8,1,8]{2,1,0:T(1,128)} %bitcast.16), calls=%async_computation | async-start | bytes 8192 | tf_op jit(solution)/shard_map/all_to_all | solution.py:71
  15.1 645.1 %all-gather.2.cloned.1.call-start = ((), (), s32[]{:S(2)}) async-start(), calls=%async_computation.2 | async-start | bytes 4718592 | tf_op jit(solution)/shard_map/all_gather | solution.py:104
  41.9 46.3 %collective-permute-start = (bf16[1,8,512,256]{3,2,1,0:T(8,128)(2,1)}, bf16[1,8,512,256]{3,2,1,0:T(8,128)(2,1)}, u32[]{:S(2)}, u32[]{:S(2)}) collective-permute-start(bf16[1,8,512,256]{3,2,1,0:T(8,128)(2,1)} %get-tuple-element.106), channel_id=1, source_target_pairs={{0,4},{4,0},{8,12},{12,8},{16,20},{20,16},{24,28},{28,24},{1,5},{5... | collective-permute-start | bytes 6291464 | tf_op jit(solution)/shard_map/ppermute | solution.py:78
  42.4 135.4 %collective-permute-start.1 = (bf16[1,8,512,256]{3,2,1,0:T(8,128)(2,1)}, bf16[1,8,512,256]{3,2,1,0:T(8,128)(2,1)}, u32[]{:S(2)}, u32[]{:S(2)}) collective-permute-start(bf16[1,8,512,256]{3,2,1,0:T(8,128)(2,1)} %get-tuple-element.105), channel_id=1, source_target_pairs={{0,8},{4,12},{8,0},{12,4},{16,24},{20,28},{24,16},{28,20},{1,9},{5... | collective-permute-start | bytes 6291464 | tf_op jit(solution)/shard_map/ppermute | solution.py:78
  43.0 178.3 %collective-permute-start.2 = (bf16[1,8,512,256]{3,2,1,0:T(8,128)(2,1)}, bf16[1,8,512,256]{3,2,1,0:T(8,128)(2,1)}, u32[]{:S(2)}, u32[]{:S(2)}) collective-permute-start(bf16[1,8,512,256]{3,2,1,0:T(8,128)(2,1)} %get-tuple-element.104), channel_id=1, source_target_pairs={{0,12},{4,8},{8,4},{12,0},{16,28},{20,24},{24,20},{28,16},{1,13},{... | collective-permute-start | bytes 6291464 | tf_op jit(solution)/shard_map/ppermute | solution.py:78
  45.4 177.6 %collective-permute-start.3 = (bf16[1,8,512,256]{3,2,1,0:T(8,128)(2,1)}, bf16[1,8,512,256]{3,2,1,0:T(8,128)(2,1)}, u32[]{:S(2)}, u32[]{:S(2)}) collective-permute-start(bf16[1,8,512,256]{3,2,1,0:T(8,128)(2,1)} %get-tuple-element.103), channel_id=1, source_target_pairs={{0,16},{4,20},{8,24},{12,28},{16,0},{20,4},{24,8},{28,12},{1,17},{... | collective-permute-start | bytes 6291464 | tf_op jit(solution)/shard_map/ppermute | solution.py:78
  45.9 273.9 %collective-permute-start.4 = (bf16[1,8,512,256]{3,2,1,0:T(8,128)(2,1)}, bf16[1,8,512,256]{3,2,1,0:T(8,128)(2,1)}, u32[]{:S(2)}, u32[]{:S(2)}) collective-permute-start(bf16[1,8,512,256]{3,2,1,0:T(8,128)(2,1)} %get-tuple-element.102), channel_id=1, source_target_pairs={{0,20},{4,16},{8,28},{12,24},{16,4},{20,0},{24,12},{28,8},{1,21},{... | collective-permute-start | bytes 6291464 | tf_op jit(solution)/shard_map/ppermute | solution.py:78
  88.2 233.4 %collective-permute-start.5 = (bf16[1,8,512,256]{3,2,1,0:T(8,128)(2,1)}, bf16[1,8,512,256]{3,2,1,0:T(8,128)(2,1)S(1)}, u32[]{:S(2)}, u32[]{:S(2)}) collective-permute-start(bf16[1,8,512,256]{3,2,1,0:T(8,128)(2,1)} %get-tuple-element.101), channel_id=1, source_target_pairs={{0,24},{4,28},{8,16},{12,20},{16,8},{20,12},{24,0},{28,4},{1,25},{... | collective-permute-start | bytes 6291464 | tf_op jit(solution)/shard_map/ppermute | solution.py:78
  177.9 143.9 %collective-permute-start.6 = (bf16[1,8,512,256]{3,2,1,0:T(8,128)(2,1)}, bf16[1,8,512,256]{3,2,1,0:T(8,128)(2,1)S(1)}, u32[]{:S(2)}, u32[]{:S(2)}) collective-permute-start(bf16[1,8,512,256]{3,2,1,0:T(8,128)(2,1)} %get-tuple-element.100), channel_id=1, source_target_pairs={{0,28},{4,24},{8,20},{12,16},{16,12},{20,8},{24,4},{28,0},{1,29},{... | collective-permute-start | bytes 6291464 | tf_op jit(solution)/shard_map/ppermute | solution.py:78
  357.8 10.9 %copy-start.1 = (bf16[256,1024]{1,0:T(8,128)(2,1)S(1)}, bf16[256,1024]{1,0:T(8,128)(2,1)}, u32[]{:S(2)}) copy-start(bf16[256,1024]{1,0:T(8,128)(2,1)} %param.8) | copy-start | bytes 1572868
  357.8 10.9 %copy-start.3 = (bf16[256,256]{1,0:T(8,128)(2,1)S(1)}, bf16[256,256]{1,0:T(8,128)(2,1)}, u32[]{:S(2)}) copy-start(bf16[256,256]{1,0:T(8,128)(2,1)} %param.9) | copy-start | bytes 393220
  504.1 206.3 %reduce-scatter.2.cloned.1.call-start = ((), (), s32[]{:S(2)}) async-start(), calls=%async_computation.3 | async-start | bytes 5242880 | tf_op jit(solution)/shard_map/reduce_scatter | solution.py:106
  712.6 41.2 %collective-permute-start.7 = (bf16[256,1024]{1,0:T(8,128)(2,1)}, bf16[256,1024]{1,0:T(8,128)(2,1)S(1)}, u32[]{:S(2)}, u32[]{:S(2)}) collective-permute-start(bf16[256,1024]{1,0:T(8,128)(2,1)} %get-tuple-element.108), channel_id=1, source_target_pairs={{0,0},{1,8},{2,16},{3,24},{4,4},{5,12},{6,20},{7,28},{8,1},{9,9},{... | collective-permute-start | bytes 1572872 | tf_op jit(solution)/shard_map/ppermute | solution.py:121
  718.1 47.5 %collective-permute-start.8 = (bf16[256,1024]{1,0:T(8,128)(2,1)}, bf16[256,1024]{1,0:T(8,128)(2,1)S(1)}, u32[]{:S(2)}, u32[]{:S(2)}) collective-permute-start(bf16[256,1024]{1,0:T(8,128)(2,1)} %get-tuple-element.107), channel_id=1, source_target_pairs={{0,4},{1,12},{2,20},{3,28},{4,0},{5,8},{6,16},{7,24},{8,5},{9,13},... | collective-permute-start | bytes 1572872 | tf_op jit(solution)/shard_map/ppermute | solution.py:121
  753.9 11.6 %copy-start.2 = (bf16[256,2048]{1,0:T(8,128)(2,1)}, bf16[256,2048]{1,0:T(8,128)(2,1)S(1)}, u32[]{:S(2)}) copy-start(bf16[256,2048]{1,0:T(8,128)(2,1)S(1)} %constant_dynamic-update-slice_fusion.1) | copy-start | bytes 3145732
Sparse Core Ops, SparseCore 0:
  504.2 155.9 all-gather.1
  668.7 41.6 reduce-scatter.1
